TPU v7x, 32 devices: a whole 2x2x4 slice. The times are simulated.
32 devices in a mesh: segment: 2 (over core), expert: 16 (over z, y, x).
Axes of the slice: x: 2, y: 2, z: 4, core: 2. Of those that a mesh axis runs over, the one named last changes fastest.
Arguments:
- hidden_in: bfloat16 [2, 256, 7168], P('segment', 'expert'), may hold values from -6 to 6
- norm_gain: bfloat16 [2, 7168], P('segment'), may hold values from 0.25 to 1.75
- up_proj: bfloat16 [2, 8192, 7168], P('segment', 'expert'), may hold values from -0.0625 to 0.0625
- down_proj: bfloat16 [2, 8192, 7168], P('segment', 'expert'), may hold values from -0.1875 to 0.1875
- expert_ids: int32 [2, 256, 2], P('segment', 'expert'), may hold values from 0 to 7, all different within a row; in each aligned block of 16 rows (0 to 15, 16 to 31, ..., all dimensions but the last counted through in order) at most 7 rows name the same one
- gate_weights: float32 [2, 256, 2], P('segment', 'expert'), may hold values from 0.2 to 1
Outputs:
- handed_on: bfloat16 [2, 256, 7168], P('segment', 'expert')
Inputs may be any that keep to these rules, and one draw needn't show every extreme that they name: `expert_ids`: each row names 2 different experts. Among the rows of one device in one section no expert is named by more than 7 rows, and in some device an expert is named by exactly 7.
All inputs are finite; a program needn't handle non-finite values.
Results may differ from a plain program's by a relative error of at most 0.0075.
Values may be sent and summed in bfloat16 or wider, within the bound.
No kernel may reach another device: no remote copies, remote signals or barrier semaphores. Data moves between devices by JAX's collectives and lax.ppermute only.
A program may use at most 64 MiB of HBM per device.

v0:
```python
import jax
import jax.numpy as jnp
from jax import lax
from jax.sharding import PartitionSpec as P

EXPERTS = 8
CAP = 7
SLOTS = 8


def passed_along(shard, axis, by):
    count = lax.axis_size(axis)
    return lax.ppermute(shard, axis, [(i, (i + by) % count) for i in range(count)])


def shards(hidden_in, norm_gain, up_proj, down_proj, expert_ids, gate_weights):
    members = lax.axis_size("expert")
    per_group = members // EXPERTS
    tokens = hidden_in[0]
    gain = norm_gain[0]
    up_block = up_proj[0]
    down_block = down_proj[0]
    routes = expert_ids[0]
    weights = gate_weights[0]
    rows_here, width = tokens.shape
    top = routes.shape[1]
    stacked, chosen = lax.optimization_barrier(
        (
            jnp.concatenate([tokens, gain[None, :]], axis=0).astype(jnp.float32),
            (routes[:, :, None] == jnp.arange(EXPERTS)[None, None, :]).astype(jnp.int32),
        )
    )
    wide = stacked[:rows_here]
    square = jnp.mean(wide**2, axis=-1, keepdims=True)
    normed = (wide * lax.rsqrt(square + 1e-06) * stacked[rows_here:]).astype(jnp.bfloat16)
    named = jnp.sum(chosen, axis=1)
    positions = jnp.arange(rows_here)
    earlier = (positions[None, :] < positions[:, None]).astype(jnp.int32)
    before = jnp.dot(earlier, named, preferred_element_type=jnp.int32)
    places = jnp.arange(EXPERTS)[None, None, :] * SLOTS + before[:, None, :]
    key = jnp.sum(chosen * places, axis=2)
    slot = jnp.arange(members * SLOTS)
    slot_device = slot % members
    slot_rank = slot // members
    slot_expert = slot_device // per_group
    hits = key[None, :, :] == (slot_expert * SLOTS + slot_rank)[:, None, None]
    picker = jnp.any(hits, axis=2).astype(jnp.bfloat16)
    outgoing = jnp.dot(picker, normed, preferred_element_type=jnp.float32).astype(jnp.bfloat16)
    outgoing = outgoing.reshape(SLOTS, members, width)
    incoming = lax.all_to_all(outgoing, "expert", split_axis=1, concat_axis=1, tiled=True)
    inner = jnp.einsum("psd,fd->psf", incoming, up_block, preferred_element_type=jnp.float32)
    active = jax.nn.silu(inner).astype(jnp.bfloat16)
    active = lax.optimization_barrier(active.transpose(1, 0, 2).reshape(members * SLOTS, -1))
    partial = jnp.dot(active, down_block, preferred_element_type=jnp.float32).astype(jnp.bfloat16)
    partial = partial.reshape(members, SLOTS, width)
    returned = lax.all_to_all(partial, "expert", split_axis=0, concat_axis=0, tiled=True).transpose(
        1, 0, 2
    )
    combine = jnp.sum(jnp.where(hits, weights[None, :, :], 0.0), axis=2).T.reshape(
        rows_here, SLOTS, members
    )
    combine_hi = combine.astype(jnp.bfloat16)
    combine_lo = (combine - combine_hi.astype(jnp.float32)).astype(jnp.bfloat16)
    mixture = jnp.einsum("rps,psd->rd", combine_hi, returned, preferred_element_type=jnp.float32)
    mixture = mixture + jnp.einsum(
        "rps,psd->rd", combine_lo, returned, preferred_element_type=jnp.float32
    )
    section_out = (tokens.astype(jnp.float32) + mixture).astype(jnp.bfloat16)
    handed = passed_along(section_out, "segment", 1)
    return handed[None]


def solution(mesh):
    in_specs = (
        P("segment", "expert", None),
        P("segment", None),
        P("segment", "expert", None),
        P("segment", "expert", None),
        P("segment", "expert", None),
        P("segment", "expert", None),
    )
    out_specs = P("segment", "expert", None)
    return jax.shard_map(shards, mesh=mesh, in_specs=in_specs, out_specs=out_specs, check_vma=False)
```

profile of v0, /device:TPU:13, one launch (start us, length us, event | category | flops | bytes accessed | tf_op | source)
XLA Modules:
  0.0 109.0 jit_solution(2199640007725550292)
XLA Ops:
  0.0 0.7 fusion.20
  0.7 1.0 maximum_convert_fusion
  1.7 0.2 multiply_reduce_fusion
  1.9 0.1 convolution_add_fusion
  2.0 0.1 multiply_reduce_fusion.1
  2.1 0.1 compare_reduce_fusion
  2.2 0.0 copy-start
  2.2 0.7 convolution_convert_fusion.1
  2.8 1.0 copy.30
  3.9 0.0 slice-start
  3.9 48.2 %all_to_all.10 = bf16[8,16,7168]{2,0,1:T(8,128)(2,1)S(1)} all-to-all(bf16[8,16,7168]{2,0,1:T(8,128)(2,1)S(1)} %copy.30), channel_id=1, replica_groups=mesh['segment'=2,'expert'=16] {'expert'}, dimensions={1} | all-to-all | bytes 3670016 | tf_op jit(solution)/shard_map/all_to_all | solution.py:50
  52.0 0.0 copy-done
  52.0 0.0 slice-start.1
  52.1 2.5 %fusion.14 = bf16[128,512]{1,0:T(8,128)(2,1)S(1)} fusion(bf16[8,16,7168]{2,0,1:T(8,128)(2,1)S(1)} %all_to_all.10, bf16[1,512,7168]{2,1,0:T(8,128)(2,1)S(1)} %copy-done), kind=kOutput, calls=%fused_computation.19 | convolution fusion | flops 939851776 | bytes 9306112 | tf_op jit(solution)/shard_map/psd,fd->psf/dot_general | solution.py:51
  54.6 0.0 slice-done
  54.6 0.0 slice-done.1
  54.6 2.4 %fusion = bf16[16,8,7168]{2,1,0:T(8,128)(2,1)} fusion(bf16[128,512]{1,0:T(8,128)(2,1)S(1)} %fusion.14, bf16[1,512,7168]{2,1,0:T(8,128)(2,1)S(1)} %bitcast.53), kind=kOutput, calls=%fused_computation.2 | convolution fusion | flops 940441600 | bytes 9306112 | tf_op jit(solution)/shard_map/dot_general | solution.py:54
  57.0 0.0 copy-start.2
  57.0 5.2 %all-to-all-start.1 = ((bf16[16,8,7168]{2,1,0:T(8,128)(2,1)}), bf16[16,8,7168]{2,1,0:T(8,128)(2,1)S(1)}, u32[]{:S(2)}, u32[]{:S(2)}) async-start(bf16[16,8,7168]{2,1,0:T(8,128)(2,1)} %fusion), calls=%async_computation.1 | async-start | bytes 3670016 | tf_op jit(solution)/shard_map/all_to_all | solution.py:56
  62.2 0.0 copy-start.1
  62.2 0.0 copy-done.2
  62.2 0.1 fusion.19
  62.3 0.1 reshape.68
  62.4 0.1 copy.32
  62.5 0.1 copy.31
  62.6 42.2 %all-to-all-done.1 = bf16[16,8,7168]{2,1,0:T(8,128)(2,1)S(1)} async-done(((bf16[16,8,7168]{2,1,0:T(8,128)(2,1)}), bf16[16,8,7168]{2,1,0:T(8,128)(2,1)S(1)}, u32[]{:S(2)}, u32[]{:S(2)}) %all-to-all-start.1) | async-done | bytes 1835040 | tf_op jit(solution)/shard_map/all_to_all | solution.py:56
  104.8 0.4 convolution_bitcast_fusion
  105.2 0.0 copy-done.1
  105.2 0.4 fusion.3
  105.7 1.5 %collective-permute-start = (bf16[16,7168]{1,0:T(8,128)(2,1)S(1)}, bf16[16,7168]{1,0:T(8,128)(2,1)S(1)}, u32[]{:S(2)}, u32[]{:S(2)}) collective-permute-start(bf16[16,7168]{1,0:T(8,128)(2,1)S(1)} %fusion.3), channel_id=1, source_target_pairs={{0,16},{16,0},{1,17},{17,1},{2,18},{18,2},{3,19},{19,3},{4,20},{20... | collective-permute-start | bytes 688136 | tf_op jit(solution)/shard_map/ppermute | solution.py:13
  107.2 1.1 %collective-permute-done = bf16[16,7168]{1,0:T(8,128)(2,1)S(1)} collective-permute-done((bf16[16,7168]{1,0:T(8,128)(2,1)S(1)}, bf16[16,7168]{1,0:T(8,128)(2,1)S(1)}, u32[]{:S(2)}, u32[]{:S(2)}) %collective-permute-start) | collective-permute-done | bytes 229408 | tf_op jit(solution)/shard_map/ppermute | solution.py:13
  108.3 0.7 copy.34
  (7 shorter events, 0.1 us)
Async XLA Ops:
  2.2 49.9 %copy-start = (bf16[1,512,7168]{2,1,0:T(8,128)(2,1)S(1)}, bf16[1,512,7168]{2,1,0:T(8,128)(2,1)}, u32[]{:S(2)}) copy-start(bf16[1,512,7168]{2,1,0:T(8,128)(2,1)} %param.8) | copy-start | bytes 22020100
  3.9 50.7 %slice-start = ((s8[7340032]{0:T(1024)(128)(4,1)}), s8[4194304]{0:T(1024)(128)(4,1)S(1)}, s32[]{:S(2)}) async-start(s8[7340032]{0:T(1024)(128)(4,1)} %bitcast.52), calls=%async_computation.2 | async-start | bytes 8388608
  52.0 2.6 %slice-start.1 = ((s8[7340032]{0:T(1024)(128)(4,1)}), s8[3145728]{0:T(1024)(128)(4,1)S(1)}, s32[]{:S(2)}) async-start(s8[7340032]{0:T(1024)(128)(4,1)} %bitcast.52), calls=%async_computation.3 | async-start | bytes 6291456
  57.0 5.2 %copy-start.2 = (f32[1,16,2]{1,2,0:T(2,128)S(1)}, f32[1,16,2]{1,2,0:T(2,128)}, u32[]{:S(2)}) copy-start(f32[1,16,2]{1,2,0:T(2,128)} %param.11) | copy-start | bytes 388
  57.0 47.8 %all-to-all-start.1 = ((bf16[16,8,7168]{2,1,0:T(8,128)(2,1)}), bf16[16,8,7168]{2,1,0:T(8,128)(2,1)S(1)}, u32[]{:S(2)}, u32[]{:S(2)}) async-start(bf16[16,8,7168]{2,1,0:T(8,128)(2,1)} %fusion), calls=%async_computation.1 | async-start | bytes 3670016 | tf_op jit(solution)/shard_map/all_to_all | solution.py:56
  62.2 43.0 %copy-start.1 = (bf16[1,16,7168]{2,1,0:T(8,128)(2,1)S(1)}, bf16[1,16,7168]{2,1,0:T(8,128)(2,1)}, u32[]{:S(2)}) copy-start(bf16[1,16,7168]{2,1,0:T(8,128)(2,1)} %param.6) | copy-start | bytes 688132
  105.7 2.6 %collective-permute-start = (bf16[16,7168]{1,0:T(8,128)(2,1)S(1)}, bf16[16,7168]{1,0:T(8,128)(2,1)S(1)}, u32[]{:S(2)}, u32[]{:S(2)}) collective-permute-start(bf16[16,7168]{1,0:T(8,128)(2,1)S(1)} %fusion.3), channel_id=1, source_target_pairs={{0,16},{16,0},{1,17},{17,1},{2,18},{18,2},{3,19},{19,3},{4,20},{20... | collective-permute-start | bytes 688136 | tf_op jit(solution)/shard_map/ppermute | solution.py:13
where the time goes:
time: 109 us
  blocking collectives  48.2 us (44%)
  waiting for transfers between devices  43.3 us (40%)
  starting transfers between devices  6.71 us (6%)
  matrix products  6.51 us (6%)
  other arithmetic  2.12 us (2%)
  local copies, waits for them, and re-layouts  2.05 us (2%)
    all_to_all x1, blocking collectives, shards(): lax.all_to_all(outgoing, 'expert', split_axis=1, concat_axis=1, tiled=True)  48.2 us
    all_to_all x1, waiting for transfers between devices, shards(): lax.all_to_all(partial, 'expert', split_axis=0, concat_axis=0, tiled=True)  42.2 us
    all_to_all x1, starting transfers between devices, shards(): lax.all_to_all(partial, 'expert', split_axis=0, concat_axis=0, tiled=True)  5.18 us
    dot_general x1, matrix products, shards(): jnp.einsum('psd,fd->psf', incoming, up_block, preferred_element_type=jnp....  2.54 us
    dot_general x1, matrix products, shards(): jnp.dot(active, down_block, preferred_element_type=jnp.float32)  2.38 us
  transfers between devices with their start and end apart: 2, of which 2 were waited for; matrix products, arithmetic and copies ran while one was open for 0% of the time, Pallas kernels for 0%

commit v1 on v0

--- a/solution.py
+++ b/solution.py
@@ -47,7 +47,12 @@
     picker = jnp.any(hits, axis=2).astype(jnp.bfloat16)
     outgoing = jnp.dot(picker, normed, preferred_element_type=jnp.float32).astype(jnp.bfloat16)
     outgoing = outgoing.reshape(SLOTS, members, width)
-    incoming = lax.all_to_all(outgoing, "expert", split_axis=1, concat_axis=1, tiled=True)
+    incoming = jnp.concatenate(
+        lax.all_to_all(
+            jnp.stack(jnp.split(outgoing, lax.axis_size("expert"), axis=1)), "expert", 0, 0
+        ),
+        axis=1,
+    )
     inner = jnp.einsum("psd,fd->psf", incoming, up_block, preferred_element_type=jnp.float32)
     active = jax.nn.silu(inner).astype(jnp.bfloat16)
     active = lax.optimization_barrier(active.transpose(1, 0, 2).reshape(members * SLOTS, -1))

time: 109 us -> 113 us (1.037)
  local copies, waits for them, and re-layouts: 2.05 us -> 5.73 us
    split x0 -> x1, local copies, waits for them, and re-layouts: none -> 4.03 us  [shards(): jnp.split(outgoing, lax.axis_size('expert'), axis=1)]
where the time goes in v1:
time: 113 us
  blocking collectives  48.2 us (43%)
  waiting for transfers between devices  43.3 us (38%)
  starting transfers between devices  6.71 us (6%)
  matrix products  6.53 us (6%)
  local copies, waits for them, and re-layouts  5.73 us (5%)
  other arithmetic  2.12 us (2%)
    all_to_all x1, blocking collectives, shards(): lax.all_to_all(jnp.stack(jnp.split(outgoing, lax.axis_size('expert'), axi...  48.2 us
    all_to_all x1, waiting for transfers between devices, shards(): lax.all_to_all(partial, 'expert', split_axis=0, concat_axis=0, tiled=True)  42.2 us
    all_to_all x1, starting transfers between devices, shards(): lax.all_to_all(partial, 'expert', split_axis=0, concat_axis=0, tiled=True)  5.18 us
    split x1, local copies, waits for them, and re-layouts, shards(): jnp.split(outgoing, lax.axis_size('expert'), axis=1)  4.03 us
    dot_general x1, matrix products, shards(): jnp.einsum('psd,fd->psf', incoming, up_block, preferred_element_type=jnp....  2.55 us
    dot_general x1, matrix products, shards(): jnp.dot(active, down_block, preferred_element_type=jnp.float32)  2.4 us
  transfers between devices with their start and end apart: 2, of which 2 were waited for; matrix products, arithmetic and copies ran while one was open for 0% of the time, Pallas kernels for 0%

profile of v1, /device:TPU:13, one launch (start us, length us, event | category | flops | bytes accessed | tf_op | source)
XLA Modules:
  0.0 112.8 jit_solution(6267057299949990083)
XLA Ops:
  0.0 0.7 fusion.43
  0.7 1.0 maximum_convert_fusion
  1.7 0.2 multiply_reduce_fusion
  1.9 0.1 convolution_add_fusion
  2.0 0.1 multiply_reduce_fusion.1
  2.1 0.1 compare_reduce_fusion
  2.2 0.7 convolution_convert_fusion.1
  2.8 0.0 slice-start
  2.9 4.0 %fusion.45 = (bf16[8,1,7168]{2,1,0:T(2,128)(2,1)S(1)}, bf16[8,1,7168]{2,1,0:T(2,128)(2,1)S(1)}, bf16[8,1,7168]{2,1,0:T(2,128)(2,1)S(1)}, bf16[8,1,7168]{2,1,0:T(...) fusion(bf16[8,16,7168]{2,1,0:T(8,128)(2,1)S(1)} %bitcast.132), kind=kLoop, calls=%fused_computation.75 | loop fusion | bytes 3670016 | tf_op jit(solution)/shard_map/split | solution.py:52
  7.0 0.0 slice-start.1
  7.7 0.0 slice-start.2
  7.7 48.2 %all_to_all.10 = bf16[16,8,1,7168]{3,1,2,0:T(8,128)(2,1)S(1)} all-to-all(bf16[16,8,1,7168]{3,1,2,0:T(8,128)(2,1)S(1)} %fusion.26), channel_id=1, replica_groups=mesh['segment'=2,'expert'=16] {'expert'}, dimensions={0} | all-to-all | bytes 3670016 | tf_op jit(solution)/shard_map/all_to_all | solution.py:51
  55.9 0.0 slice-done
  55.9 0.0 slice-done.1
  55.9 0.0 slice-start.3
  55.9 2.5 %fusion.19 = bf16[128,512]{1,0:T(8,128)(2,1)S(1)} fusion(bf16[1,512,7168]{2,1,0:T(8,128)(2,1)S(1)} %bitcast.129, bf16[16,8,1,7168]{3,1,2,0:T(8,128)(2,1)S(1)} %all_to_all.10), kind=kOutput, calls=%fused_computation.20 | convolution fusion | flops 939851776 | bytes 9306112 | tf_op jit(solution)/shard_map/psd,fd->psf/dot_general | solution.py:56
  58.4 0.0 slice-done.2
  58.4 0.0 slice-done.3
  58.5 2.4 %fusion = bf16[16,8,7168]{2,1,0:T(8,128)(2,1)} fusion(bf16[128,512]{1,0:T(8,128)(2,1)S(1)} %fusion.19, bf16[1,512,7168]{2,1,0:T(8,128)(2,1)S(1)} %bitcast.131), kind=kOutput, calls=%fused_computation.2 | convolution fusion | flops 940441600 | bytes 9306112 | tf_op jit(solution)/shard_map/dot_general | solution.py:59
  60.9 0.0 copy-start.1
  60.9 5.2 %all-to-all-start.1 = ((bf16[16,8,7168]{2,1,0:T(8,128)(2,1)}), bf16[16,8,7168]{2,1,0:T(8,128)(2,1)S(1)}, u32[]{:S(2)}, u32[]{:S(2)}) async-start(bf16[16,8,7168]{2,1,0:T(8,128)(2,1)} %fusion), calls=%async_computation.1 | async-start | bytes 3670016 | tf_op jit(solution)/shard_map/all_to_all | solution.py:61
  66.0 0.0 copy-start
  66.0 0.0 copy-done.1
  66.1 0.1 fusion.42
  66.1 0.1 reshape.74
  66.2 0.1 copy.127
  66.4 0.1 copy.126
  66.5 42.2 %all-to-all-done.1 = bf16[16,8,7168]{2,1,0:T(8,128)(2,1)S(1)} async-done(((bf16[16,8,7168]{2,1,0:T(8,128)(2,1)}), bf16[16,8,7168]{2,1,0:T(8,128)(2,1)S(1)}, u32[]{:S(2)}, u32[]{:S(2)}) %all-to-all-start.1) | async-done | bytes 1835040 | tf_op jit(solution)/shard_map/all_to_all | solution.py:61
  108.7 0.4 convolution_bitcast_fusion
  109.1 0.0 copy-done
  109.1 0.4 fusion.3
  109.5 1.5 %collective-permute-start = (bf16[16,7168]{1,0:T(8,128)(2,1)S(1)}, bf16[16,7168]{1,0:T(8,128)(2,1)S(1)}, u32[]{:S(2)}, u32[]{:S(2)}) collective-permute-start(bf16[16,7168]{1,0:T(8,128)(2,1)S(1)} %fusion.3), channel_id=1, source_target_pairs={{0,16},{16,0},{1,17},{17,1},{2,18},{18,2},{3,19},{19,3},{4,20},{20... | collective-permute-start | bytes 688136 | tf_op jit(solution)/shard_map/ppermute | solution.py:13
  111.0 1.1 collective-permute-done
  112.1 0.7 copy.208
  (24 shorter events, 0.7 us)
Async XLA Ops:
  2.8 53.0 %slice-start = ((s8[7340032]{0:T(1024)(128)(4,1)}), s8[4194304]{0:T(1024)(128)(4,1)S(1)}, s32[]{:S(2)}) async-start(s8[7340032]{0:T(1024)(128)(4,1)} %bitcast.128), calls=%async_computation.2 | async-start | bytes 8388608
  7.0 48.9 %slice-start.1 = ((s8[7340032]{0:T(1024)(128)(4,1)}), s8[3145728]{0:T(1024)(128)(4,1)S(1)}, s32[]{:S(2)}) async-start(s8[7340032]{0:T(1024)(128)(4,1)} %bitcast.128), calls=%async_computation.3 | async-start | bytes 6291456
  7.7 50.7 %slice-start.2 = ((s8[7340032]{0:T(1024)(128)(4,1)}), s8[4194304]{0:T(1024)(128)(4,1)S(1)}, s32[]{:S(2)}) async-start(s8[7340032]{0:T(1024)(128)(4,1)} %bitcast.130), calls=%async_computation.4 | async-start | bytes 8388608
  55.9 2.6 %slice-start.3 = ((s8[7340032]{0:T(1024)(128)(4,1)}), s8[3145728]{0:T(1024)(128)(4,1)S(1)}, s32[]{:S(2)}) async-start(s8[7340032]{0:T(1024)(128)(4,1)} %bitcast.130), calls=%async_computation.5 | async-start | bytes 6291456
  60.9 5.2 %copy-start.1 = (f32[1,16,2]{1,2,0:T(2,128)S(1)}, f32[1,16,2]{1,2,0:T(2,128)}, u32[]{:S(2)}) copy-start(f32[1,16,2]{1,2,0:T(2,128)} %param.11) | copy-start | bytes 388
  60.9 47.8 %all-to-all-start.1 = ((bf16[16,8,7168]{2,1,0:T(8,128)(2,1)}), bf16[16,8,7168]{2,1,0:T(8,128)(2,1)S(1)}, u32[]{:S(2)}, u32[]{:S(2)}) async-start(bf16[16,8,7168]{2,1,0:T(8,128)(2,1)} %fusion), calls=%async_computation.1 | async-start | bytes 3670016 | tf_op jit(solution)/shard_map/all_to_all | solution.py:61
  66.0 43.0 %copy-start = (bf16[1,16,7168]{2,1,0:T(8,128)(2,1)S(1)}, bf16[1,16,7168]{2,1,0:T(8,128)(2,1)}, u32[]{:S(2)}) copy-start(bf16[1,16,7168]{2,1,0:T(8,128)(2,1)} %param.6) | copy-start | bytes 688132
  109.5 2.6 %collective-permute-start = (bf16[16,7168]{1,0:T(8,128)(2,1)S(1)}, bf16[16,7168]{1,0:T(8,128)(2,1)S(1)}, u32[]{:S(2)}, u32[]{:S(2)}) collective-permute-start(bf16[16,7168]{1,0:T(8,128)(2,1)S(1)} %fusion.3), channel_id=1, source_target_pairs={{0,16},{16,0},{1,17},{17,1},{2,18},{18,2},{3,19},{19,3},{4,20},{20... | collective-permute-start | bytes 688136 | tf_op jit(solution)/shard_map/ppermute | solution.py:13
